TPU v7x, 32 devices: a whole 2x2x4 slice. The times are simulated.
32 devices in a mesh: groups: 2 (over y), seq: 8 (over z, x), head: 2 (over core).
Axes of the slice: x: 2, y: 2, z: 4, core: 2. Of those that a mesh axis runs over, the one named last changes fastest.
Arguments:
- query_vectors: bfloat16 [2, 16384, 512], P(None, ('groups', 'seq'), 'head'), parts along dimension 1, may hold values from -8 to 8
- key_vectors: bfloat16 [2, 16384, 512], P(None, ('groups', 'seq'), 'head'), parts along dimension 1, may hold values from -8 to 8
- value_vectors: bfloat16 [2, 16384, 512], P(None, ('groups', 'seq'), 'head'), parts along dimension 1, may hold values from -12 to 12
Outputs:
- attended: bfloat16 [2, 16384, 512], P(None, ('groups', 'seq'), 'head'), parts along dimension 1
There are 2 independent parts, one for each index of `groups`. A program takes and returns all parts, laid end to end along the dimension named above; each array names one. Nothing has to cross between parts.
All inputs are finite; a program needn't handle non-finite values.
Results may differ from a plain program's by a relative error of at most 0.0039.
Values may be sent and summed in bfloat16 or wider, within the bound.
No kernel may reach another device: no remote copies, remote signals or barrier semaphores. Data moves between devices by JAX's collectives and lax.ppermute only.
A program may use at most 64 MiB of HBM per device.

v0:
```python
import math
import jax
import jax.numpy as jnp
from jax import lax
from jax.sharding import PartitionSpec as P

DH = 128
STRIDE = 1024


def shifted(block, axis, distance):
    devices = range(lax.axis_size(axis))
    route = [(i - distance, i) for i in devices if i - distance in devices]
    return lax.ppermute(block, axis, route)


def attend_columns(query_cols, key_cols, value_cols):
    score_scale = 1.0 / math.sqrt(DH)
    scores = (
        jnp.einsum("rchd,schd->chrs", query_cols, key_cols, preferred_element_type=jnp.float32)
        * score_scale
    )
    count = query_cols.shape[0]
    row_pos = jnp.arange(count, dtype=jnp.int32)[:, None]
    other_pos = jnp.arange(count, dtype=jnp.int32)[None, :]
    allowed = other_pos <= row_pos
    scores = jnp.where(allowed[None, None], scores, -jnp.inf)
    maxima = jnp.max(scores, axis=-1, keepdims=True)
    expo = jnp.exp(scores - maxima)
    weights = (expo / jnp.sum(expo, axis=-1, keepdims=True)).astype(jnp.bfloat16)
    return jnp.einsum(
        "chrs,schd->rchd", weights, value_cols, preferred_element_type=jnp.float32
    ).astype(jnp.bfloat16)


def local(query_vectors, key_vectors, value_vectors):
    local_tokens = query_vectors.shape[1]
    feature_width = query_vectors.shape[2]
    heads_here = feature_width // DH
    rows_here = local_tokens // STRIDE
    score_scale = 1.0 / math.sqrt(DH)
    prev_keys, prev_values = shifted(
        (key_vectors[0, local_tokens - STRIDE :], value_vectors[0, local_tokens - STRIDE :]),
        "seq",
        1,
    )
    ext_keys = jnp.concatenate([prev_keys, key_vectors[0]], axis=0).reshape(
        local_tokens + STRIDE, heads_here, DH
    )
    ext_values = jnp.concatenate([prev_values, value_vectors[0]], axis=0).reshape(
        local_tokens + STRIDE, heads_here, DH
    )
    queries = query_vectors[0].reshape(local_tokens, heads_here, DH)
    block_size = min(512, local_tokens)
    first_token = lax.axis_index("seq") * local_tokens

    def one_block(offset):
        query_block = lax.dynamic_slice_in_dim(queries, offset, block_size, 0)
        key_block = lax.dynamic_slice_in_dim(ext_keys, offset, STRIDE + block_size, 0)
        value_block = lax.dynamic_slice_in_dim(ext_values, offset, STRIDE + block_size, 0)
        scores = (
            jnp.einsum("qhd,khd->hqk", query_block, key_block, preferred_element_type=jnp.float32)
            * score_scale
        )
        query_pos = jnp.arange(block_size, dtype=jnp.int32)[:, None]
        key_pos = jnp.arange(STRIDE + block_size, dtype=jnp.int32)[None, :]
        allowed = (
            (key_pos > query_pos)
            & (key_pos <= STRIDE + query_pos)
            & (first_token + offset + key_pos >= STRIDE)
        )
        scores = jnp.where(allowed[None], scores, -jnp.inf)
        maxima = jnp.max(scores, axis=-1, keepdims=True)
        expo = jnp.exp(scores - maxima)
        weights = (expo / jnp.sum(expo, axis=-1, keepdims=True)).astype(jnp.bfloat16)
        return jnp.einsum(
            "hqk,khd->qhd", weights, value_block, preferred_element_type=jnp.float32
        ).astype(jnp.bfloat16)

    starts = jnp.arange(local_tokens // block_size, dtype=jnp.int32) * block_size
    row_out = lax.map(one_block, starts).reshape(local_tokens, feature_width)
    query_grid = query_vectors[1].reshape(rows_here, STRIDE, heads_here, DH)
    key_grid = key_vectors[1].reshape(rows_here, STRIDE, heads_here, DH)
    value_grid = value_vectors[1].reshape(rows_here, STRIDE, heads_here, DH)
    result = attend_columns(
        lax.all_to_all(query_grid, "seq", split_axis=1, concat_axis=0, tiled=True),
        lax.all_to_all(key_grid, "seq", split_axis=1, concat_axis=0, tiled=True),
        lax.all_to_all(value_grid, "seq", split_axis=1, concat_axis=0, tiled=True),
    )
    context = lax.all_to_all(result, "seq", split_axis=0, concat_axis=1, tiled=True)
    column_out = context.reshape(local_tokens, feature_width)
    return jnp.stack([row_out, column_out])


def solution(mesh):
    return jax.shard_map(
        local,
        mesh=mesh,
        in_specs=(
            P(None, ("groups", "seq"), "head"),
            P(None, ("groups", "seq"), "head"),
            P(None, ("groups", "seq"), "head"),
        ),
        out_specs=P(None, ("groups", "seq"), "head"),
        check_vma=False,
    )
```

profile of v0, /device:TPU:0, one launch (start us, length us, event | category | flops | bytes accessed | tf_op | source)
XLA Modules:
  0.0 122.1 jit_solution(14857121246988676300)
XLA Ops:
  0.0 1.3 %fusion.63 = (bf16[1,1024,256]{2,1,0:T(8,128)(2,1)S(1)}, bf16[1,1024,256]{2,1,0:T(8,128)(2,1)S(1)}) fusion(bf16[2,1024,256]{2,1,0:T(8,128)(2,1)} %param.5), kind=kLoop, calls=%fused_computation.57 | loop fusion | bytes 2097152 | tf_op jit(solution)/shard_map/slice | solution.py:53
  1.3 0.2 copy.98
  1.5 0.0 copy-start
  1.5 1.1 copy.71
  2.6 7.3 %all-to-all-start = ((bf16[1,1024,2,128]{3,2,0,1:T(2,128)(2,1)}), bf16[1,1024,2,128]{3,2,0,1:T(2,128)(2,1)S(1)}, u32[]{:S(2)}, u32[]{:S(2)}) async-start(bf16[1,1024,2,128]{3,2,0,1:T(2,128)(2,1)} %copy.71), calls=%async_computation | async-start | bytes 1048576 | tf_op jit(solution)/shard_map/all_to_all | solution.py:86
  9.9 0.9 fusion.62
  10.7 0.2 copy.99
  10.9 1.1 copy.74
  12.0 12.3 %all-to-all-done = bf16[1,1024,2,128]{3,2,0,1:T(2,128)(2,1)S(1)} async-done(((bf16[1,1024,2,128]{3,2,0,1:T(2,128)(2,1)}), bf16[1,1024,2,128]{3,2,0,1:T(2,128)(2,1)S(1)}, u32[]{:S(2)}, u32[]{:S(2)}) %all-to-all-start) | async-done | bytes 524320 | tf_op jit(solution)/shard_map/all_to_all | solution.py:86
  24.3 3.6 %all-to-all-start.1 = ((bf16[1,1024,2,128]{3,2,0,1:T(2,128)(2,1)}), bf16[1,1024,2,128]{3,2,0,1:T(2,128)(2,1)S(1)}, u32[]{:S(2)}, u32[]{:S(2)}) async-start(bf16[1,1024,2,128]{3,2,0,1:T(2,128)(2,1)} %copy.74), calls=%async_computation.1 | async-start | bytes 1048576 | tf_op jit(solution)/shard_map/all_to_all | solution.py:87
  28.0 2.1 %slice_bitcast_fusion = (bf16[1024,256]{1,0:T(8,128)(2,1)}, bf16[1,1024,256]{2,1,0:T(8,128)(2,1)S(1)}, bf16[1,1024,256]{2,1,0:T(8,128)(2,1)S(1)}) fusion(bf16[2,1024,256]{2,1,0:T(8,128)(2,1)} %param.7), kind=kLoop, calls=%fused_computation.54 | loop fusion | bytes 2621440 | tf_op jit(solution)/shard_map/squeeze | solution.py:43
  30.1 4.7 %collective-permute-start = (bf16[1024,256]{1,0:T(8,128)(2,1)}, bf16[1024,256]{1,0:T(8,128)(2,1)}, u32[]{:S(2)}, u32[]{:S(2)}) collective-permute-start(bf16[1024,256]{1,0:T(8,128)(2,1)} %get-tuple-element.89), channel_id=1, source_target_pairs={{0,2},{2,4},{4,6},{6,8},{8,10},{10,12},{12,14},{1,3},{3,5},{5,7},{... | collective-permute-start | bytes 1572872 | tf_op jit(solution)/shard_map/ppermute | solution.py:14
  34.8 1.2 %copy.97 = bf16[1,1024,256]{1,2,0:T(8,128)(2,1)S(1)} copy(bf16[1,1024,256]{2,1,0:T(8,128)(2,1)} %get-tuple-element.85) | data formatting | bytes 1048576
  36.0 3.4 %collective-permute-start.1 = (bf16[1024,256]{0,1:T(8,128)(2,1)S(1)}, bf16[1024,256]{0,1:T(8,128)(2,1)}, u32[]{:S(2)}, u32[]{:S(2)}) collective-permute-start(bf16[1024,256]{0,1:T(8,128)(2,1)S(1)} %bitcast.36), channel_id=1, source_target_pairs={{0,2},{2,4},{4,6},{6,8},{8,10},{10,12},{12,14},{1,3},{3,5},{5,7},{... | collective-permute-start | bytes 1572872 | tf_op jit(solution)/shard_map/ppermute | solution.py:14
  39.4 1.0 copy.96
  40.4 0.2 copy.100
  40.7 1.1 copy.80
  41.8 0.2 copy.64
  42.0 5.5 %collective-permute-done = bf16[1024,256]{1,0:T(8,128)(2,1)} collective-permute-done((bf16[1024,256]{1,0:T(8,128)(2,1)}, bf16[1024,256]{1,0:T(8,128)(2,1)}, u32[]{:S(2)}, u32[]{:S(2)}) %collective-permute-start) | collective-permute-done | bytes 524320 | tf_op jit(solution)/shard_map/ppermute | solution.py:14
  47.5 1.2 %copy.63 = bf16[1024,256]{0,1:T(8,128)(2,1)S(1)} copy(bf16[1024,256]{1,0:T(8,128)(2,1)} %collective-permute-done) | data formatting | bytes 1048576 | tf_op jit(solution)/shard_map/ppermute | solution.py:14
  48.7 9.1 %collective-permute-done.1 = bf16[1024,256]{0,1:T(8,128)(2,1)} collective-permute-done((bf16[1024,256]{0,1:T(8,128)(2,1)S(1)}, bf16[1024,256]{0,1:T(8,128)(2,1)}, u32[]{:S(2)}, u32[]{:S(2)}) %collective-permute-start.1) | collective-permute-done | bytes 524320 | tf_op jit(solution)/shard_map/ppermute | solution.py:14
  57.8 2.1 %pad_maximum_fusion.1 = bf16[2048,2,128]{0,2,1:T(8,128)(2,1)} fusion(bf16[1024,2,128]{0,2,1:T(8,128)(2,1)S(1)} %bitcast.37, bf16[1024,2,128]{0,2,1:T(8,128)(2,1)} %bitcast.8), kind=kLoop, calls=%fused_computation.38 | loop fusion | flops 2097152 | bytes 2097152 | tf_op jit(solution)/shard_map/concatenate | solution.py:47
  59.9 10.2 %all-to-all-start.2 = ((bf16[1,1024,2,128]{3,2,0,1:T(2,128)(2,1)}), bf16[1,1024,2,128]{3,2,0,1:T(2,128)(2,1)S(1)}, u32[]{:S(2)}, u32[]{:S(2)}) async-start(bf16[1,1024,2,128]{3,2,0,1:T(2,128)(2,1)} %copy.80), calls=%async_computation.2 | async-start | bytes 1048576 | tf_op jit(solution)/shard_map/all_to_all | solution.py:88
  70.1 1.1 pad_maximum_fusion
  71.2 0.7 fusion.48
  71.8 0.4 copy.78
  72.3 0.8 fusion.64
  73.1 0.4 copy.82
  73.6 11.2 %all-to-all-done.2 = bf16[1,1024,2,128]{3,2,0,1:T(2,128)(2,1)S(1)} async-done(((bf16[1,1024,2,128]{3,2,0,1:T(2,128)(2,1)}), bf16[1,1024,2,128]{3,2,0,1:T(2,128)(2,1)S(1)}, u32[]{:S(2)}, u32[]{:S(2)}) %all-to-all-start.2) | async-done | bytes 524320 | tf_op jit(solution)/shard_map/all_to_all | solution.py:88
  84.8 0.5 fusion.44
  85.2 0.0 copy-start.2
  85.3 1.2 copy.84
  86.4 3.7 %all-to-all-start.3 = ((bf16[8,128,2,128]{3,2,1,0:T(2,128)(2,1)}), bf16[8,128,2,128]{3,2,1,0:T(2,128)(2,1)S(1)}, u32[]{:S(2)}, u32[]{:S(2)}) async-start(bf16[8,128,2,128]{3,2,1,0:T(2,128)(2,1)} %copy.84), calls=%async_computation.3 | async-start | bytes 1048576 | tf_op jit(solution)/shard_map/all_to_all | solution.py:90
  90.1 28.0 %while.10 = (s32[]{:T(128)}, bf16[2,512,2,128]{1,3,2,0:T(8,128)(2,1)}, s32[2]{0:T(128)S(1)}, bf16[2048,2,128]{0,2,1:T(8,128)(2,1)S(1)}, s32[]{:T(128)}, /*index=...) while((s32[]{:T(128)}, ...), condition=%wide.region_3.4_spmd, body=%wide.region_0.3_spmd.sunk | while | flops 1225399808 | bytes 5522644 | solution.py:81
  90.2 0.6 dynamic_slice.50
  94.7 0.6 fusion.79
  95.3 3.6 %fusion.80 = f32[2,512]{1,0:T(2,128)S(1)} fusion(pred[512,1536]{1,0:T(8,128)(4,1)S(1)} %fusion.79, bf16[2048,2,128]{0,2,1:T(8,128)(2,1)S(1)} %get-tuple-element.165, s32[]{:T(128)S(6)} %select_n.38, bf16[1024,2,128]{0,2,1:T(8,128)(2,1)} %get-tuple-element.164, s32[]{:T(128)S(6)} %select_n.39), kind=kOutput, calls=%fused_computation.55.clone.1 | convolution fusion | flops 408946176 | bytes 1839112 | tf_op jit(solution)/shard_map/while/body/eval_jaxpr/sub | solution.py:74
  98.9 5.3 %fusion.81 = bf16[2,512,2,128]{1,3,2,0:T(8,128)(2,1)} fusion(bf16[2,512,2,128]{1,3,2,0:T(8,128)(2,1)} %get-tuple-element.149, s32[]{:T(128)S(6)} %copy.110, f32[2,512]{1,0:T(2,128)S(1)} %fusion.80, bf16[2048,2,128]{0,2,1:T(8,128)(2,1)S(1)} %get-tuple-element.162, s32[]{:T(128)S(6)} %select_n.38, pred[512,1536]{1,0:T(8,128)(4,1)S(1)} %fusion.79, ...), kind=kOutput, calls=%fused_computation.15.clone.1 | convolution fusion | flops 813304320 | bytes 2889728 | tf_op jit(solution)/shard_map/while/body/eval_jaxpr/hqk,khd->qhd/dot_general | solution.py:76
  104.2 0.6 dynamic_slice.50
  108.6 0.6 fusion.79
  109.3 3.6 %fusion.80 = f32[2,512]{1,0:T(2,128)S(1)} fusion(pred[512,1536]{1,0:T(8,128)(4,1)S(1)} %fusion.79, bf16[2048,2,128]{0,2,1:T(8,128)(2,1)S(1)} %get-tuple-element.165, s32[]{:T(128)S(6)} %select_n.38, bf16[1024,2,128]{0,2,1:T(8,128)(2,1)} %get-tuple-element.164, s32[]{:T(128)S(6)} %select_n.39), kind=kOutput, calls=%fused_computation.55.clone.1 | convolution fusion | flops 408946176 | bytes 1839112 | tf_op jit(solution)/shard_map/while/body/eval_jaxpr/sub | solution.py:74
  112.9 5.3 %fusion.81 = bf16[2,512,2,128]{1,3,2,0:T(8,128)(2,1)} fusion(bf16[2,512,2,128]{1,3,2,0:T(8,128)(2,1)} %get-tuple-element.149, s32[]{:T(128)S(6)} %copy.110, f32[2,512]{1,0:T(2,128)S(1)} %fusion.80, bf16[2048,2,128]{0,2,1:T(8,128)(2,1)S(1)} %get-tuple-element.162, s32[]{:T(128)S(6)} %select_n.38, pred[512,1536]{1,0:T(8,128)(4,1)S(1)} %fusion.79, ...), kind=kOutput, calls=%fused_computation.15.clone.1 | convolution fusion | flops 813304320 | bytes 2889728 | tf_op jit(solution)/shard_map/while/body/eval_jaxpr/hqk,khd->qhd/dot_general | solution.py:76
  118.2 1.6 %copy.69 = bf16[2,512,2,128]{1,0,3,2:T(2,128)(2,1)S(1)} copy(bf16[2,512,2,128]{1,3,2,0:T(8,128)(2,1)} %get-tuple-element.42) | data formatting | bytes 1048576 | tf_op jit(solution)/shard_map/while | solution.py:81
  119.7 0.4 stack_reshape.6
  120.1 0.3 reshape.96
  120.5 0.2 copy.93
  120.7 0.1 pad_maximum_fusion.2
  120.8 1.3 %copy.86 = bf16[2,1024,256]{2,1,0:T(8,128)(2,1)} copy(bf16[2,1024,256]{1,2,0:T(8,128)(2,1)S(1)} %pad_maximum_fusion.2) | data formatting | bytes 2097152 | tf_op jit(solution)/shard_map/stack | solution.py:92
  (14 shorter events, 0.1 us)
Async XLA Ops:
  1.5 8.4 %copy-start = (bf16[2,1024,256]{2,1,0:T(8,128)(2,1)S(1)}, bf16[2,1024,256]{2,1,0:T(8,128)(2,1)}, u32[]{:S(2)}) copy-start(bf16[2,1024,256]{2,1,0:T(8,128)(2,1)} %param.6) | copy-start | bytes 3145732
  2.6 21.7 %all-to-all-start = ((bf16[1,1024,2,128]{3,2,0,1:T(2,128)(2,1)}), bf16[1,1024,2,128]{3,2,0,1:T(2,128)(2,1)S(1)}, u32[]{:S(2)}, u32[]{:S(2)}) async-start(bf16[1,1024,2,128]{3,2,0,1:T(2,128)(2,1)} %copy.71), calls=%async_computation | async-start | bytes 1048576 | tf_op jit(solution)/shard_map/all_to_all | solution.py:86
  24.3 35.5 %all-to-all-start.1 = ((bf16[1,1024,2,128]{3,2,0,1:T(2,128)(2,1)}), bf16[1,1024,2,128]{3,2,0,1:T(2,128)(2,1)S(1)}, u32[]{:S(2)}, u32[]{:S(2)}) async-start(bf16[1,1024,2,128]{3,2,0,1:T(2,128)(2,1)} %copy.74), calls=%async_computation.1 | async-start | bytes 1048576 | tf_op jit(solution)/shard_map/all_to_all | solution.py:87
  30.1 17.4 %collective-permute-start = (bf16[1024,256]{1,0:T(8,128)(2,1)}, bf16[1024,256]{1,0:T(8,128)(2,1)}, u32[]{:S(2)}, u32[]{:S(2)}) collective-permute-start(bf16[1024,256]{1,0:T(8,128)(2,1)} %get-tuple-element.89), channel_id=1, source_target_pairs={{0,2},{2,4},{4,6},{6,8},{8,10},{10,12},{12,14},{1,3},{3,5},{5,7},{... | collective-permute-start | bytes 1572872 | tf_op jit(solution)/shard_map/ppermute | solution.py:14
  36.0 21.7 %collective-permute-start.1 = (bf16[1024,256]{0,1:T(8,128)(2,1)S(1)}, bf16[1024,256]{0,1:T(8,128)(2,1)}, u32[]{:S(2)}, u32[]{:S(2)}) collective-permute-start(bf16[1024,256]{0,1:T(8,128)(2,1)S(1)} %bitcast.36), channel_id=1, source_target_pairs={{0,2},{2,4},{4,6},{6,8},{8,10},{10,12},{12,14},{1,3},{3,5},{5,7},{... | collective-permute-start | bytes 1572872 | tf_op jit(solution)/shard_map/ppermute | solution.py:14
  59.9 24.9 %all-to-all-start.2 = ((bf16[1,1024,2,128]{3,2,0,1:T(2,128)(2,1)}), bf16[1,1024,2,128]{3,2,0,1:T(2,128)(2,1)S(1)}, u32[]{:S(2)}, u32[]{:S(2)}) async-start(bf16[1,1024,2,128]{3,2,0,1:T(2,128)(2,1)} %copy.80), calls=%async_computation.2 | async-start | bytes 1048576 | tf_op jit(solution)/shard_map/all_to_all | solution.py:88
  85.2 4.9 %copy-start.1 = (bf16[2048,2,128]{0,2,1:T(8,128)(2,1)S(1)}, bf16[2048,2,128]{0,2,1:T(8,128)(2,1)}, u32[]{:S(2)}) copy-start(bf16[2048,2,128]{0,2,1:T(8,128)(2,1)} %pad_maximum_fusion.1) | copy-start | bytes 3145732
  85.2 4.9 %copy-start.2 = (bf16[2048,2,128]{0,2,1:T(8,128)(2,1)S(1)}, bf16[2048,2,128]{0,2,1:T(8,128)(2,1)}, u32[]{:S(2)}) copy-start(bf16[2048,2,128]{0,2,1:T(8,128)(2,1)} %pad_maximum_fusion) | copy-start | bytes 3145732
  86.4 33.7 %all-to-all-start.3 = ((bf16[8,128,2,128]{3,2,1,0:T(2,128)(2,1)}), bf16[8,128,2,128]{3,2,1,0:T(2,128)(2,1)S(1)}, u32[]{:S(2)}, u32[]{:S(2)}) async-start(bf16[8,128,2,128]{3,2,1,0:T(2,128)(2,1)} %copy.84), calls=%async_computation.3 | async-start | bytes 1048576 | tf_op jit(solution)/shard_map/all_to_all | solution.py:90
where the time goes:
time: 123 us; the launch traced here: 122 us
  waiting for transfers between devices  38 us (31%)
  starting transfers between devices  32.9 us (27%)
  local copies, waits for them, and re-layouts  18.9 us (15%)
  matrix products  18.9 us (15%)
  loops' own time  7.82 us (6%)
  other arithmetic  5.39 us (4%)
    ppermute x2, waiting for transfers between devices, shifted(): return lax.ppermute(block, axis, route)  14.5 us
    all_to_all x1, waiting for transfers between devices, local(): lax.all_to_all(query_grid, 'seq', split_axis=1, concat_axis=0, tiled=True)  12.3 us
    all_to_all x1, waiting for transfers between devices, local(): lax.all_to_all(value_grid, 'seq', split_axis=1, concat_axis=0, tiled=True)  11.2 us
    dot_general x2, matrix products, one_block(): jnp.einsum('hqk,khd->qhd', weights, value_block, preferred_element_type=j...  10.6 us
    all_to_all x1, starting transfers between devices, local(): lax.all_to_all(value_grid, 'seq', split_axis=1, concat_axis=0, tiled=True)  10.2 us
    ppermute x2, starting transfers between devices, shifted(): return lax.ppermute(block, axis, route)  8.12 us
    another operation x1, loops' own time, local(): row_out = lax.map(one_block, starts).reshape(local_tokens, feature_width)  7.82 us
    all_to_all x1, starting transfers between devices, local(): lax.all_to_all(query_grid, 'seq', split_axis=1, concat_axis=0, tiled=True)  7.25 us
  transfers between devices with their start and end apart: 6, of which 4 were waited for; matrix products, arithmetic and copies ran while one was open for 30% of the time, Pallas kernels for 0%

commit v1 on v0

--- a/solution.py
+++ b/solution.py
@@ -6,6 +6,28 @@
 
 DH = 128
 STRIDE = 1024
+
+
+def in_blocks(x, dim, size):
+    before, after = (x.shape[:dim], x.shape[dim + 1 :])
+    return jnp.moveaxis(x.reshape(*before, size, -1, *after), dim, 0)
+
+
+def joined_along(blocks, dim):
+    shape = list(blocks.shape[1:])
+    shape[dim] *= blocks.shape[0]
+    return jnp.moveaxis(blocks, 0, dim).reshape(shape)
+
+
+def pairwise_exchange(x, axis, split_dim, concat_dim):
+    size, index = (lax.axis_size(axis), lax.axis_index(axis))
+    blocks = in_blocks(x, split_dim, size)
+    outs = [blocks[index]]
+    for step in range(1, size):
+        sent = blocks[index ^ step]
+        outs.append(lax.ppermute(sent, axis, [(i, i ^ step) for i in range(size)]))
+    blocks = jnp.stack(outs)[index ^ jnp.arange(size)]
+    return joined_along(blocks, concat_dim)
 
 
 def shifted(block, axis, distance):
@@ -83,7 +105,7 @@
     key_grid = key_vectors[1].reshape(rows_here, STRIDE, heads_here, DH)
     value_grid = value_vectors[1].reshape(rows_here, STRIDE, heads_here, DH)
     result = attend_columns(
-        lax.all_to_all(query_grid, "seq", split_axis=1, concat_axis=0, tiled=True),
+        pairwise_exchange(query_grid, "seq", 1, 0),
         lax.all_to_all(key_grid, "seq", split_axis=1, concat_axis=0, tiled=True),
         lax.all_to_all(value_grid, "seq", split_axis=1, concat_axis=0, tiled=True),
     )

time: 123 us -> 110 us (0.89)
  waiting for transfers between devices: 38 us -> 14.8 us
  starting transfers between devices: 32.9 us -> 39.2 us
  local copies, waits for them, and re-layouts: 18.9 us -> 22.8 us
    ppermute x0 -> x7, starting transfers between devices: none -> 14.2 us  [pairwise_exchange(): outs.append(lax.ppermute(sent, axis, [(i, i ^ step) for i in range(size)]))]
    all_to_all x1 -> x0, waiting for transfers between devices: 12.3 us -> none  [local(): lax.all_to_all(query_grid, 'seq', split_axis=1, concat_axis=0, tiled=True)]
    all_to_all x1 -> x0, starting transfers between devices: 7.25 us -> none  [local(): lax.all_to_all(query_grid, 'seq', split_axis=1, concat_axis=0, tiled=True)]
    ppermute x2, waiting for transfers between devices: 14.5 us -> 8.52 us  [shifted(): return lax.ppermute(block, axis, route)]
    all_to_all x1, waiting for transfers between devices: 11.2 us -> 6.27 us  [local(): lax.all_to_all(value_grid, 'seq', split_axis=1, concat_axis=0, tiled=True)]
    all_to_all x1, starting transfers between devices: 3.67 us -> 7.01 us  [local(): lax.all_to_all(result, 'seq', split_axis=0, concat_axis=1, tiled=True)]
    dynamic_slice x0 -> x8, local copies, waits for them, and re-layouts: none -> 2.97 us  [pairwise_exchange(): sent = blocks[index ^ step]]
    all_to_all x1, starting transfers between devices: 10.2 us -> 7.39 us  [local(): lax.all_to_all(value_grid, 'seq', split_axis=1, concat_axis=0, tiled=True)]
  transfers between devices with their start and end apart: 6 -> 12, of which waited for: 4 -> 3; matrix products, arithmetic and copies ran while one was open for 30% -> 38% of each run, Pallas kernels for 0% -> 0%
where the time goes in v1:
time: 110 us; the launch traced here: 109 us
  starting transfers between devices  39.2 us (36%)
  local copies, waits for them, and re-layouts  22.8 us (21%)
  matrix products  18.9 us (17%)
  waiting for transfers between devices  14.8 us (13%)
  loops' own time  7.82 us (7%)
  other arithmetic  5.41 us (5%)
    ppermute x7, starting transfers between devices, pairwise_exchange(): outs.append(lax.ppermute(sent, axis, [(i, i ^ step) for i in range(size)]))  14.2 us
    dot_general x2, matrix products, one_block(): jnp.einsum('hqk,khd->qhd', weights, value_block, preferred_element_type=j...  10.6 us
    ppermute x2, waiting for transfers between devices, shifted(): return lax.ppermute(block, axis, route)  8.52 us
    another operation x1, loops' own time, local(): row_out = lax.map(one_block, starts).reshape(local_tokens, feature_width)  7.82 us
    all_to_all x1, starting transfers between devices, local(): lax.all_to_all(value_grid, 'seq', split_axis=1, concat_axis=0, tiled=True)  7.39 us
    sub x2, matrix products, one_block(): expo = jnp.exp(scores - maxima)  7.12 us
    all_to_all x1, starting transfers between devices, local(): lax.all_to_all(result, 'seq', split_axis=0, concat_axis=1, tiled=True)  7.01 us
    all_to_all x1, waiting for transfers between devices, local(): lax.all_to_all(value_grid, 'seq', split_axis=1, concat_axis=0, tiled=True)  6.27 us
  transfers between devices with their start and end apart: 12, of which 3 were waited for; matrix products, arithmetic and copies ran while one was open for 38% of the time, Pallas kernels for 0%

profile of v1, /device:TPU:0, one launch (start us, length us, event | category | flops | bytes accessed | tf_op | source)
XLA Modules:
  0.0 109.3 jit_solution(15931970521250855006)
XLA Ops:
  0.0 1.3 %fusion.64 = (bf16[1,1024,256]{2,1,0:T(8,128)(2,1)S(1)}, bf16[1,1024,256]{2,1,0:T(8,128)(2,1)S(1)}) fusion(bf16[2,1024,256]{2,1,0:T(8,128)(2,1)} %param.5), kind=kLoop, calls=%fused_computation.84 | loop fusion | bytes 2097152 | tf_op jit(solution)/shard_map/slice | solution.py:75
  1.9 0.6 copy.154
  2.5 2.9 %collective-permute-start.2 = (bf16[1,128,2,128]{3,1,2,0:T(8,128)(2,1)}, bf16[1,128,2,128]{3,1,2,0:T(8,128)(2,1)}, u32[]{:S(2)}, u32[]{:S(2)}) collective-permute-start(bf16[1,128,2,128]{3,1,2,0:T(8,128)(2,1)} %bitcast.61), channel_id=1, source_target_pairs={{0,2},{2,0},{4,6},{6,4},{8,10},{10,8},{12,14},{14,12},{1,3},{3,1},... | collective-permute-start | bytes 196616 | tf_op jit(solution)/shard_map/ppermute | solution.py:28
  5.4 0.6 copy.153
  6.1 1.6 %collective-permute-start.3 = (bf16[1,128,2,128]{3,1,2,0:T(8,128)(2,1)}, bf16[1,128,2,128]{3,1,2,0:T(8,128)(2,1)}, u32[]{:S(2)}, u32[]{:S(2)}) collective-permute-start(bf16[1,128,2,128]{3,1,2,0:T(8,128)(2,1)} %bitcast.60), channel_id=1, source_target_pairs={{0,4},{2,6},{4,0},{6,2},{8,12},{10,14},{12,8},{14,10},{1,5},{3,7},... | collective-permute-start | bytes 196616 | tf_op jit(solution)/shard_map/ppermute | solution.py:28
  7.7 0.6 copy.152
  8.3 0.6 copy.151
  8.9 3.0 %collective-permute-start.5 = (bf16[1,128,2,128]{3,1,2,0:T(8,128)(2,1)}, bf16[1,128,2,128]{3,1,2,0:T(8,128)(2,1)S(1)}, u32[]{:S(2)}, u32[]{:S(2)}) collective-permute-start(bf16[1,128,2,128]{3,1,2,0:T(8,128)(2,1)} %bitcast.58), channel_id=1, source_target_pairs={{0,8},{2,10},{4,12},{6,14},{8,0},{10,2},{12,4},{14,6},{1,9},{3,11}... | collective-permute-start | bytes 196616 | tf_op jit(solution)/shard_map/ppermute | solution.py:28
  11.9 1.3 %collective-permute-start.6 = (bf16[1,128,2,128]{3,1,2,0:T(8,128)(2,1)S(1)}, bf16[1,128,2,128]{3,1,2,0:T(8,128)(2,1)S(1)}, u32[]{:S(2)}, u32[]{:S(2)}) collective-permute-start(bf16[1,128,2,128]{3,1,2,0:T(8,128)(2,1)S(1)} %bitcast.76), channel_id=1, source_target_pairs={{0,10},{2,8},{4,14},{6,12},{8,2},{10,0},{12,6},{14,4},{1,11},{3,9}... | collective-permute-start | bytes 196616 | tf_op jit(solution)/shard_map/ppermute | solution.py:28
  13.6 1.1 %copy.93 = bf16[1,1024,2,128]{3,2,0,1:T(2,128)(2,1)} copy(bf16[1,1024,2,128]{1,3,2,0:T(8,128)(2,1)S(1)} %bitcast.67) | data formatting | bytes 1048576 | tf_op jit(solution)/shard_map/reshape;squeeze | solution.py:105
  14.7 4.9 %all-to-all-start = ((bf16[1,1024,2,128]{3,2,0,1:T(2,128)(2,1)}), bf16[1,1024,2,128]{3,2,0,1:T(2,128)(2,1)S(1)}, u32[]{:S(2)}, u32[]{:S(2)}) async-start(bf16[1,1024,2,128]{3,2,0,1:T(2,128)(2,1)} %copy.93), calls=%async_computation | async-start | bytes 1048576 | tf_op jit(solution)/shard_map/all_to_all | solution.py:109
  19.6 0.6 copy_dynamic-update-slice_fusion
  20.3 2.1 %slice_bitcast_fusion = (bf16[1024,256]{1,0:T(8,128)(2,1)}, bf16[1,1024,256]{2,1,0:T(8,128)(2,1)S(1)}, bf16[1,1024,256]{2,1,0:T(8,128)(2,1)S(1)}) fusion(bf16[2,1024,256]{2,1,0:T(8,128)(2,1)} %param.7), kind=kLoop, calls=%fused_computation.81 | loop fusion | bytes 2621440 | tf_op jit(solution)/shard_map/squeeze | solution.py:65
  22.6 1.1 %copy.99 = bf16[1,1024,2,128]{3,2,0,1:T(2,128)(2,1)} copy(bf16[1,1024,2,128]{1,3,2,0:T(8,128)(2,1)S(1)} %bitcast.68) | data formatting | bytes 1048576 | tf_op jit(solution)/shard_map/reshape;squeeze | solution.py:106
  24.1 1.0 copy.115
  25.2 3.8 %collective-permute-start.7 = (bf16[1,128,2,128]{3,1,2,0:T(8,128)(2,1)S(1)}, bf16[1,128,2,128]{3,1,2,0:T(8,128)(2,1)S(1)}, u32[]{:S(2)}, u32[]{:S(2)}) collective-permute-start(bf16[1,128,2,128]{3,1,2,0:T(8,128)(2,1)S(1)} %bitcast.78), channel_id=1, source_target_pairs={{0,12},{2,14},{4,8},{6,10},{8,4},{10,6},{12,0},{14,2},{1,13},{3,15... | collective-permute-start | bytes 196616 | tf_op jit(solution)/shard_map/ppermute | solution.py:28
  29.0 0.9 bitcast_dynamic-update-slice_fusion.6
  29.8 1.5 %collective-permute-start.8 = (bf16[1,128,2,128]{3,1,2,0:T(8,128)(2,1)S(1)}, bf16[1,128,2,128]{3,1,2,0:T(8,128)(2,1)S(1)}, u32[]{:S(2)}, u32[]{:S(2)}) collective-permute-start(bf16[1,128,2,128]{3,1,2,0:T(8,128)(2,1)S(1)} %bitcast.77), channel_id=1, source_target_pairs={{0,14},{2,12},{4,10},{6,8},{8,6},{10,4},{12,2},{14,0},{1,15},{3,13... | collective-permute-start | bytes 196616 | tf_op jit(solution)/shard_map/ppermute | solution.py:28
  31.4 0.9 bitcast_dynamic-update-slice_fusion.5
  32.2 2.7 %collective-permute-start = (bf16[1024,256]{1,0:T(8,128)(2,1)}, bf16[1024,256]{1,0:T(8,128)(2,1)}, u32[]{:S(2)}, u32[]{:S(2)}) collective-permute-start(bf16[1024,256]{1,0:T(8,128)(2,1)} %get-tuple-element.89), channel_id=1, source_target_pairs={{0,2},{2,4},{4,6},{6,8},{8,10},{10,12},{12,14},{1,3},{3,5},{5,7},{... | collective-permute-start | bytes 1572872 | tf_op jit(solution)/shard_map/ppermute | solution.py:36
  35.0 0.9 bitcast_dynamic-update-slice_fusion.4
  35.8 3.1 %collective-permute-start.1 = (bf16[1024,256]{0,1:T(8,128)(2,1)S(1)}, bf16[1024,256]{0,1:T(8,128)(2,1)}, u32[]{:S(2)}, u32[]{:S(2)}) collective-permute-start(bf16[1024,256]{0,1:T(8,128)(2,1)S(1)} %bitcast.70), channel_id=1, source_target_pairs={{0,2},{2,4},{4,6},{6,8},{8,10},{10,12},{12,14},{1,3},{3,5},{5,7},{... | collective-permute-start | bytes 1572872 | tf_op jit(solution)/shard_map/ppermute | solution.py:36
  39.0 0.6 gather_fusion
  39.6 7.7 %collective-permute-done = bf16[1024,256]{1,0:T(8,128)(2,1)} collective-permute-done((bf16[1024,256]{1,0:T(8,128)(2,1)}, bf16[1024,256]{1,0:T(8,128)(2,1)}, u32[]{:S(2)}, u32[]{:S(2)}) %collective-permute-start) | collective-permute-done | bytes 524320 | tf_op jit(solution)/shard_map/ppermute | solution.py:36
  47.4 1.2 %copy.76 = bf16[1024,256]{0,1:T(8,128)(2,1)S(1)} copy(bf16[1024,256]{1,0:T(8,128)(2,1)} %collective-permute-done) | data formatting | bytes 1048576 | tf_op jit(solution)/shard_map/ppermute | solution.py:36
  48.6 1.1 pad_maximum_fusion
  49.7 7.4 %all-to-all-start.1 = ((bf16[1,1024,2,128]{3,2,0,1:T(2,128)(2,1)}), bf16[1,1024,2,128]{3,2,0,1:T(2,128)(2,1)S(1)}, u32[]{:S(2)}, u32[]{:S(2)}) async-start(bf16[1,1024,2,128]{3,2,0,1:T(2,128)(2,1)} %copy.99), calls=%async_computation.1 | async-start | bytes 1048576 | tf_op jit(solution)/shard_map/all_to_all | solution.py:110
  57.1 0.8 collective-permute-done.1
  57.9 2.1 %pad_maximum_fusion.1 = bf16[2048,2,128]{0,2,1:T(8,128)(2,1)} fusion(bf16[1024,2,128]{0,2,1:T(8,128)(2,1)S(1)} %bitcast.71, bf16[1024,2,128]{0,2,1:T(8,128)(2,1)} %bitcast.8), kind=kLoop, calls=%fused_computation.39 | loop fusion | flops 2097152 | bytes 2097152 | tf_op jit(solution)/shard_map/concatenate | solution.py:69
  60.0 0.7 fusion.48
  60.6 0.4 copy.97
  61.1 0.8 fusion.65
  61.9 0.4 copy.101
  62.4 6.3 %all-to-all-done.1 = bf16[1,1024,2,128]{3,2,0,1:T(2,128)(2,1)S(1)} async-done(((bf16[1,1024,2,128]{3,2,0,1:T(2,128)(2,1)}), bf16[1,1024,2,128]{3,2,0,1:T(2,128)(2,1)S(1)}, u32[]{:S(2)}, u32[]{:S(2)}) %all-to-all-start.1) | async-done | bytes 524320 | tf_op jit(solution)/shard_map/all_to_all | solution.py:110
  68.6 0.5 fusion.44
  69.1 1.2 %copy.103 = bf16[8,128,2,128]{3,2,1,0:T(2,128)(2,1)} copy(bf16[8,128,2,128]{3,0,2,1:T(8,128)(2,1)S(1)} %fusion.44) | data formatting | bytes 1048576 | tf_op jit(solution)/shard_map/convert_element_type | solution.py:55
  70.3 7.0 %all-to-all-start.2 = ((bf16[8,128,2,128]{3,2,1,0:T(2,128)(2,1)}), bf16[8,128,2,128]{3,2,1,0:T(2,128)(2,1)S(1)}, u32[]{:S(2)}, u32[]{:S(2)}) async-start(bf16[8,128,2,128]{3,2,1,0:T(2,128)(2,1)} %copy.103), calls=%async_computation.2 | async-start | bytes 1048576 | tf_op jit(solution)/shard_map/all_to_all | solution.py:112
  77.4 28.0 %while.10 = (s32[]{:T(128)}, bf16[2,512,2,128]{1,3,2,0:T(8,128)(2,1)}, s32[2]{0:T(128)S(1)}, bf16[2048,2,128]{0,2,1:T(8,128)(2,1)S(1)}, s32[]{:T(128)}, /*index=...) while((s32[]{:T(128)}, ...), condition=%wide.region_3.4_spmd, body=%wide.region_0.3_spmd.sunk | while | flops 1225399808 | bytes 5522636 | solution.py:103
  77.4 0.6 dynamic_slice.90
  81.9 0.6 fusion.80
  82.5 3.6 %fusion.81 = f32[2,512]{1,0:T(2,128)S(1)} fusion(pred[512,1536]{1,0:T(8,128)(4,1)S(1)} %fusion.80, bf16[2048,2,128]{0,2,1:T(8,128)(2,1)S(1)} %get-tuple-element.173, s32[]{:T(128)S(6)} %select_n.84, bf16[1024,2,128]{0,2,1:T(8,128)(2,1)} %get-tuple-element.172, s32[]{:T(128)S(6)} %select_n.85), kind=kOutput, calls=%fused_computation.82.clone.1 | convolution fusion | flops 408946176 | bytes 1839112 | tf_op jit(solution)/shard_map/while/body/eval_jaxpr/sub | solution.py:96
  86.1 5.3 %fusion.82 = bf16[2,512,2,128]{1,3,2,0:T(8,128)(2,1)} fusion(bf16[2,512,2,128]{1,3,2,0:T(8,128)(2,1)} %get-tuple-element.157, s32[]{:T(128)} %get-tuple-element.156, f32[2,512]{1,0:T(2,128)S(1)} %fusion.81, bf16[2048,2,128]{0,2,1:T(8,128)(2,1)S(1)} %get-tuple-element.170, s32[]{:T(128)S(6)} %select_n.84, pred[512,1536]{1,0:T(8,128)(4,1)S(1)} %fusion.80, ...), kind=kOutput, calls=%fused_computation.16.clone.1 | convolution fusion | flops 813304320 | bytes 2889728 | tf_op jit(solution)/shard_map/while/body/eval_jaxpr/hqk,khd->qhd/dot_general | solution.py:98
  91.3 0.6 dynamic_slice.90
  95.8 0.6 fusion.80
  96.5 3.6 %fusion.81 = f32[2,512]{1,0:T(2,128)S(1)} fusion(pred[512,1536]{1,0:T(8,128)(4,1)S(1)} %fusion.80, bf16[2048,2,128]{0,2,1:T(8,128)(2,1)S(1)} %get-tuple-element.173, s32[]{:T(128)S(6)} %select_n.84, bf16[1024,2,128]{0,2,1:T(8,128)(2,1)} %get-tuple-element.172, s32[]{:T(128)S(6)} %select_n.85), kind=kOutput, calls=%fused_computation.82.clone.1 | convolution fusion | flops 408946176 | bytes 1839112 | tf_op jit(solution)/shard_map/while/body/eval_jaxpr/sub | solution.py:96
  100.0 5.3 %fusion.82 = bf16[2,512,2,128]{1,3,2,0:T(8,128)(2,1)} fusion(bf16[2,512,2,128]{1,3,2,0:T(8,128)(2,1)} %get-tuple-element.157, s32[]{:T(128)} %get-tuple-element.156, f32[2,512]{1,0:T(2,128)S(1)} %fusion.81, bf16[2048,2,128]{0,2,1:T(8,128)(2,1)S(1)} %get-tuple-element.170, s32[]{:T(128)S(6)} %select_n.84, pred[512,1536]{1,0:T(8,128)(4,1)S(1)} %fusion.80, ...), kind=kOutput, calls=%fused_computation.16.clone.1 | convolution fusion | flops 813304320 | bytes 2889728 | tf_op jit(solution)/shard_map/while/body/eval_jaxpr/hqk,khd->qhd/dot_general | solution.py:98
  105.4 1.6 %copy.82 = bf16[2,512,2,128]{1,0,3,2:T(2,128)(2,1)S(1)} copy(bf16[2,512,2,128]{1,3,2,0:T(8,128)(2,1)} %get-tuple-element.42) | data formatting | bytes 1048576 | tf_op jit(solution)/shard_map/while | solution.py:103
  108.0 1.3 %copy.105 = bf16[2,1024,256]{2,1,0:T(8,128)(2,1)} copy(bf16[2,1024,256]{1,2,0:T(8,128)(2,1)S(1)} %pad_maximum_fusion.2) | data formatting | bytes 2097152 | tf_op jit(solution)/shard_map/stack | solution.py:114
  (46 shorter events, 2.6 us)
Async XLA Ops:
  1.4 11.9 %copy-start = (bf16[2,1024,256]{2,1,0:T(8,128)(2,1)S(1)}, bf16[2,1024,256]{2,1,0:T(8,128)(2,1)}, u32[]{:S(2)}) copy-start(bf16[2,1024,256]{2,1,0:T(8,128)(2,1)} %param.6) | copy-start | bytes 3145732
  2.5 22.7 %collective-permute-start.2 = (bf16[1,128,2,128]{3,1,2,0:T(8,128)(2,1)}, bf16[1,128,2,128]{3,1,2,0:T(8,128)(2,1)}, u32[]{:S(2)}, u32[]{:S(2)}) collective-permute-start(bf16[1,128,2,128]{3,1,2,0:T(8,128)(2,1)} %bitcast.61), channel_id=1, source_target_pairs={{0,2},{2,0},{4,6},{6,4},{8,10},{10,8},{12,14},{14,12},{1,3},{3,1},... | collective-permute-start | bytes 196616 | tf_op jit(solution)/shard_map/ppermute | solution.py:28
  6.1 23.8 %collective-permute-start.3 = (bf16[1,128,2,128]{3,1,2,0:T(8,128)(2,1)}, bf16[1,128,2,128]{3,1,2,0:T(8,128)(2,1)}, u32[]{:S(2)}, u32[]{:S(2)}) collective-permute-start(bf16[1,128,2,128]{3,1,2,0:T(8,128)(2,1)} %bitcast.60), channel_id=1, source_target_pairs={{0,4},{2,6},{4,0},{6,2},{8,12},{10,14},{12,8},{14,10},{1,5},{3,7},... | collective-permute-start | bytes 196616 | tf_op jit(solution)/shard_map/ppermute | solution.py:28
  8.3 23.9 %collective-permute-start.4 = (bf16[1,128,2,128]{3,1,2,0:T(8,128)(2,1)}, bf16[1,128,2,128]{3,1,2,0:T(8,128)(2,1)}, u32[]{:S(2)}, u32[]{:S(2)}) collective-permute-start(bf16[1,128,2,128]{3,1,2,0:T(8,128)(2,1)} %bitcast.59), channel_id=1, source_target_pairs={{0,6},{2,4},{4,2},{6,0},{8,14},{10,12},{12,10},{14,8},{1,7},{3,5},... | collective-permute-start | bytes 196616 | tf_op jit(solution)/shard_map/ppermute | solution.py:28
  8.9 26.9 %collective-permute-start.5 = (bf16[1,128,2,128]{3,1,2,0:T(8,128)(2,1)}, bf16[1,128,2,128]{3,1,2,0:T(8,128)(2,1)S(1)}, u32[]{:S(2)}, u32[]{:S(2)}) collective-permute-start(bf16[1,128,2,128]{3,1,2,0:T(8,128)(2,1)} %bitcast.58), channel_id=1, source_target_pairs={{0,8},{2,10},{4,12},{6,14},{8,0},{10,2},{12,4},{14,6},{1,9},{3,11}... | collective-permute-start | bytes 196616 | tf_op jit(solution)/shard_map/ppermute | solution.py:28
  11.9 27.0 %collective-permute-start.6 = (bf16[1,128,2,128]{3,1,2,0:T(8,128)(2,1)S(1)}, bf16[1,128,2,128]{3,1,2,0:T(8,128)(2,1)S(1)}, u32[]{:S(2)}, u32[]{:S(2)}) collective-permute-start(bf16[1,128,2,128]{3,1,2,0:T(8,128)(2,1)S(1)} %bitcast.76), channel_id=1, source_target_pairs={{0,10},{2,8},{4,14},{6,12},{8,2},{10,0},{12,6},{14,4},{1,11},{3,9}... | collective-permute-start | bytes 196616 | tf_op jit(solution)/shard_map/ppermute | solution.py:28
  14.7 35.0 %all-to-all-start = ((bf16[1,1024,2,128]{3,2,0,1:T(2,128)(2,1)}), bf16[1,1024,2,128]{3,2,0,1:T(2,128)(2,1)S(1)}, u32[]{:S(2)}, u32[]{:S(2)}) async-start(bf16[1,1024,2,128]{3,2,0,1:T(2,128)(2,1)} %copy.93), calls=%async_computation | async-start | bytes 1048576 | tf_op jit(solution)/shard_map/all_to_all | solution.py:109
  23.9 5.1 %copy-start.3 = (bf16[8,1,128,2,128]{4,2,3,0,1:T(8,128)(2,1)S(1)}, bf16[8,1,128,2,128]{4,2,3,0,1:T(8,128)(2,1)}, u32[]{:S(2)}) copy-start(bf16[8,1,128,2,128]{4,2,3,0,1:T(8,128)(2,1)} %copy_dynamic-update-slice_fusion) | copy-start | bytes 1572868
  25.2 13.8 %collective-permute-start.7 = (bf16[1,128,2,128]{3,1,2,0:T(8,128)(2,1)S(1)}, bf16[1,128,2,128]{3,1,2,0:T(8,128)(2,1)S(1)}, u32[]{:S(2)}, u32[]{:S(2)}) collective-permute-start(bf16[1,128,2,128]{3,1,2,0:T(8,128)(2,1)S(1)} %bitcast.78), channel_id=1, source_target_pairs={{0,12},{2,14},{4,8},{6,10},{8,4},{10,6},{12,0},{14,2},{1,13},{3,15... | collective-permute-start | bytes 196616 | tf_op jit(solution)/shard_map/ppermute | solution.py:28
  29.8 9.1 %collective-permute-start.8 = (bf16[1,128,2,128]{3,1,2,0:T(8,128)(2,1)S(1)}, bf16[1,128,2,128]{3,1,2,0:T(8,128)(2,1)S(1)}, u32[]{:S(2)}, u32[]{:S(2)}) collective-permute-start(bf16[1,128,2,128]{3,1,2,0:T(8,128)(2,1)S(1)} %bitcast.77), channel_id=1, source_target_pairs={{0,14},{2,12},{4,10},{6,8},{8,6},{10,4},{12,2},{14,0},{1,15},{3,13... | collective-permute-start | bytes 196616 | tf_op jit(solution)/shard_map/ppermute | solution.py:28
  32.2 15.1 %collective-permute-start = (bf16[1024,256]{1,0:T(8,128)(2,1)}, bf16[1024,256]{1,0:T(8,128)(2,1)}, u32[]{:S(2)}, u32[]{:S(2)}) collective-permute-start(bf16[1024,256]{1,0:T(8,128)(2,1)} %get-tuple-element.89), channel_id=1, source_target_pairs={{0,2},{2,4},{4,6},{6,8},{8,10},{10,12},{12,14},{1,3},{3,5},{5,7},{... | collective-permute-start | bytes 1572872 | tf_op jit(solution)/shard_map/ppermute | solution.py:36
  35.8 22.0 %collective-permute-start.1 = (bf16[1024,256]{0,1:T(8,128)(2,1)S(1)}, bf16[1024,256]{0,1:T(8,128)(2,1)}, u32[]{:S(2)}, u32[]{:S(2)}) collective-permute-start(bf16[1024,256]{0,1:T(8,128)(2,1)S(1)} %bitcast.70), channel_id=1, source_target_pairs={{0,2},{2,4},{4,6},{6,8},{8,10},{10,12},{12,14},{1,3},{3,5},{5,7},{... | collective-permute-start | bytes 1572872 | tf_op jit(solution)/shard_map/ppermute | solution.py:36
  49.7 18.9 %all-to-all-start.1 = ((bf16[1,1024,2,128]{3,2,0,1:T(2,128)(2,1)}), bf16[1,1024,2,128]{3,2,0,1:T(2,128)(2,1)S(1)}, u32[]{:S(2)}, u32[]{:S(2)}) async-start(bf16[1,1024,2,128]{3,2,0,1:T(2,128)(2,1)} %copy.99), calls=%async_computation.1 | async-start | bytes 1048576 | tf_op jit(solution)/shard_map/all_to_all | solution.py:110
  69.1 8.2 %copy-start.1 = (bf16[2048,2,128]{0,2,1:T(8,128)(2,1)S(1)}, bf16[2048,2,128]{0,2,1:T(8,128)(2,1)}, u32[]{:S(2)}) copy-start(bf16[2048,2,128]{0,2,1:T(8,128)(2,1)} %pad_maximum_fusion) | copy-start | bytes 3145732
  69.1 8.2 %copy-start.2 = (bf16[2048,2,128]{0,2,1:T(8,128)(2,1)S(1)}, bf16[2048,2,128]{0,2,1:T(8,128)(2,1)}, u32[]{:S(2)}) copy-start(bf16[2048,2,128]{0,2,1:T(8,128)(2,1)} %pad_maximum_fusion.1) | copy-start | bytes 3145732
  70.3 37.0 %all-to-all-start.2 = ((bf16[8,128,2,128]{3,2,1,0:T(2,128)(2,1)}), bf16[8,128,2,128]{3,2,1,0:T(2,128)(2,1)S(1)}, u32[]{:S(2)}, u32[]{:S(2)}) async-start(bf16[8,128,2,128]{3,2,1,0:T(2,128)(2,1)} %copy.103), calls=%async_computation.2 | async-start | bytes 1048576 | tf_op jit(solution)/shard_map/all_to_all | solution.py:112
